TPU v7x, 512 devices: a whole 4x8x8 slice. The times are simulated.
512 devices in a mesh: cfg: 2 (over y_hi), req: 8 (over y_lo, core), seq: 32 (over z, x).
Axes of the slice: x: 4, y: 8 (y_hi: 2, y_lo: 4; y = y_hi * 4 + y_lo), z: 8, core: 2. Of those that a mesh axis runs over, the one named last changes fastest.
Arguments:
- query: bfloat16 [2, 8, 1024, 768], P('cfg', 'req', 'seq'), may hold values from -6 to 6
- key_value: bfloat16 [2, 2, 8, 1280, 768], P(None, 'cfg', 'req', 'seq'), may hold values from -6 to 6
- residual_in: bfloat16 [2, 8, 1024, 1536], P('cfg', 'req', 'seq'), may hold values from -0.119628906 to 0.119628906
- text_len: int32 [2, 8], P('cfg', 'req'), may hold values from 1 to 154, as said below
- attn_gate: float32 [2, 8, 1536], P('cfg', 'req'), may hold values from 0.5 to 2
- mlp_shift: float32 [2, 8, 1536], P('cfg', 'req'), may hold values from -3 to 3
- mlp_scale: float32 [2, 8, 1536], P('cfg', 'req'), may hold values from -3 to 3
- mlp_gate: float32 [2, 8, 1536], P('cfg', 'req'), may hold values from 0.5 to 2
- shift: float32 [2, 8, 1536], P('cfg', 'req'), may hold values from -3 to 3
- scale: float32 [2, 8, 1536], P('cfg', 'req'), may hold values from -3 to 3
- w_proj: bfloat16 [768, 1536], P(None, 'req'), may hold values from -0.21875 to 0.21875
- w_up: bfloat16 [1536, 3072], P(None, 'req'), may hold values from -0.15625 to 0.15625
- w_down: bfloat16 [3072, 1536], P('req'), may hold values from -0.109375 to 0.109375
- w_out: bfloat16 [1536, 64], replicated, may hold values from -1 to 1
- latent: float32 [8, 1024, 64], P('req', 'seq', 'cfg'), may hold values from -6 to 6
- step_size: float32 [8], P('req'), may hold values from 0.1 to 0.5
Outputs:
- latent_next: float32 [8, 1024, 64], P('req', 'seq', 'cfg')
- guided_norm: float32 [8], P('req')
- peak: float32 [8], P('req')
Inputs may be any that keep to these rules, and one draw needn't show every extreme that they name: `text_len`: some entry equals 154.
All inputs are finite; a program needn't handle non-finite values.
Results may differ from a plain program's by a relative error of at most 0.015.
Values may be sent and summed in bfloat16 or wider, within the bound.
No kernel may reach another device: no remote copies, remote signals or barrier semaphores. Data moves between devices by JAX's collectives and lax.ppermute only.
A program may use at most 64 MiB of HBM per device.

v0:
```python
import jax
import jax.numpy as jnp
from jax import lax
from jax.sharding import PartitionSpec as P

HEADS = 12
HD = 64
guidance_weight = 4.0


def swapped(block, axis, apart):
    count = lax.axis_size(axis)
    route = []
    for low in range(count):
        high = low | 1 << apart
        if high != low and high < count:
            route += [(low, high), (high, low)]
    return lax.ppermute(block, axis, route)


def modulate_rows(hidden, shift_row, scale_row):
    row_mean = jnp.mean(hidden, axis=1, keepdims=True)
    centered = hidden - row_mean
    row_var = jnp.mean(centered * centered, axis=1, keepdims=True)
    return (
        centered * lax.rsqrt(row_var + 1e-06) * (1.0 + scale_row[None, :]) + shift_row[None, :]
    ).astype(jnp.bfloat16)


def per_device(
    query,
    key_value,
    residual_in,
    text_len,
    attn_gate,
    mlp_shift,
    mlp_scale,
    mlp_gate,
    shift,
    scale,
    w_proj,
    w_up,
    w_down,
    w_out,
    latent,
    step_size,
):
    img_dev = query.shape[2]
    rows_dev = key_value.shape[3]
    txt_dev = rows_dev - img_dev
    length = text_len[0, 0]
    queries = query[0, 0].reshape(img_dev, HEADS, HD)
    key_vals = key_value[:, 0, 0]
    factor = HD ** (-0.5)
    piece = lax.all_gather(key_vals, "seq", axis=1, tiled=True)
    running_max = jnp.full((img_dev, HEADS), -1e30, jnp.float32)
    piece_rows = piece.shape[1]
    positions = jnp.arange(piece_rows, dtype=jnp.int32)
    within = positions % rows_dev
    text_slot = positions // rows_dev * txt_dev + within - img_dev
    usable = ((within < img_dev) | (text_slot < length))[None, None, :]
    keys_here = piece[0].reshape(piece_rows, HEADS, HD)
    vals_here = piece[1].reshape(piece_rows, HEADS, HD)
    logits = (
        jnp.einsum("qhd,khd->qhk", queries, keys_here, preferred_element_type=jnp.float32) * factor
    )
    new_max = jnp.maximum(running_max, jnp.max(jnp.where(usable, logits, -1e30), axis=2))
    weights = jnp.where(usable, jnp.exp(logits - new_max[:, :, None]), 0.0)
    running_sum = jnp.sum(weights, axis=2)
    weighted = jnp.einsum(
        "qhk,khd->qhd", weights.astype(jnp.bfloat16), vals_here, preferred_element_type=jnp.float32
    )
    attended = (
        (weighted / running_sum[:, :, None]).reshape(img_dev, HEADS * HD).astype(jnp.bfloat16)
    )
    projected = jnp.dot(
        attended,
        lax.all_gather(w_proj, "req", axis=1, tiled=True),
        preferred_element_type=jnp.float32,
    )
    hidden = residual_in[0, 0].astype(jnp.float32) + attn_gate[0, 0][None, :] * projected
    mlp_in = modulate_rows(hidden, mlp_shift[0, 0], mlp_scale[0, 0])
    inner = jax.nn.gelu(
        jnp.dot(
            lax.all_gather(mlp_in, "req", axis=0, tiled=True),
            w_up,
            preferred_element_type=jnp.float32,
        ),
        approximate=True,
    ).astype(jnp.bfloat16)
    mlp_out = lax.psum_scatter(
        jnp.dot(inner, w_down, preferred_element_type=jnp.float32).astype(jnp.bfloat16),
        "req",
        scatter_dimension=0,
        tiled=True,
    ).astype(jnp.float32)
    hidden_two = hidden + mlp_gate[0, 0][None, :] * mlp_out
    modulated = modulate_rows(hidden_two, shift[0, 0], scale[0, 0])
    velocity = jnp.dot(modulated, w_out, preferred_element_type=jnp.float32)
    half_width = velocity.shape[1] // lax.axis_size("cfg")
    side_index = lax.axis_index("cfg")
    received = swapped(velocity, "cfg", 0)
    is_cond = side_index == 0
    cond_part = jnp.where(is_cond, velocity, received)
    uncond = jnp.where(is_cond, received, velocity)
    guided_full = uncond + guidance_weight * (cond_part - uncond)
    partials = jnp.stack([jnp.sum(guided_full * guided_full), jnp.max(jnp.abs(guided_full))])
    n_seq = lax.axis_size("seq")
    gathered = lax.all_to_all(jnp.broadcast_to(partials[None], (n_seq, 2)), "seq", 0, 0, tiled=True)
    guided_total = jnp.sum(gathered[:, 0])
    peak_value = jnp.max(gathered[:, 1])
    entries = img_dev * n_seq * velocity.shape[1]
    guided_norm = jnp.sqrt(guided_total / entries + 1e-06)
    guided = lax.dynamic_slice_in_dim(guided_full, side_index * half_width, half_width, 1)
    latent_next = latent + step_size[0] * guided[None, :, :]
    return (latent_next, jnp.reshape(guided_norm, (1,)), jnp.reshape(peak_value, (1,)))


def solution(mesh):
    in_specs = (
        P("cfg", "req", "seq", None),
        P(None, "cfg", "req", "seq", None),
        P("cfg", "req", "seq", None),
        P("cfg", "req"),
        P("cfg", "req", None),
        P("cfg", "req", None),
        P("cfg", "req", None),
        P("cfg", "req", None),
        P("cfg", "req", None),
        P("cfg", "req", None),
        P(None, "req"),
        P(None, "req"),
        P("req", None),
        P(),
        P("req", "seq", "cfg"),
        P("req"),
    )
    out_specs = (P("req", "seq", "cfg"), P("req"), P("req"))
    return jax.shard_map(
        per_device, mesh=mesh, in_specs=in_specs, out_specs=out_specs, check_vma=False
    )
```

profile of v0, /device:TPU:2, one launch (start us, length us, event | category | flops | bytes accessed | tf_op | source)
XLA Modules:
  0.0 248.8 jit_solution(4121349338983233270)
XLA Ops:
  7.2 0.7 all-gather.6.cloned.1.call-update
  8.0 0.7 all-gather.4.cloned.1.call-update
  9.4 0.9 reshape_squeeze.10
  10.3 0.7 reduce.2
  11.0 0.7 reduce.5
  11.8 0.7 add_reduce_fusion.1
  12.5 89.9 %all-gather.6.cloned.1.call-done = bf16[2,1,1,1280,768]{4,3,2,1,0:T(8,128)(2,1)} async-done(((bf16[2,1,1,40,768]{4,3,2,1,0:T(8,128)(2,1)}), bf16[2,1,1,1280,768]{4,3,2,1,0:T(8,128)(2,1)}) %all-gather.6.cloned.1.call-update) | async-done | bytes 3932176 | tf_op jit(solution)/shard_map/all_gather | solution.py:55
  102.4 4.3 %fusion.46 = (bf16[1,1,1,1280,768]{4,3,2,1,0:T(8,128)(2,1)}, bf16[1,1,1,1280,768]{4,3,2,1,0:T(8,128)(2,1)}) fusion(bf16[2,1,1,1280,768]{4,3,2,1,0:T(8,128)(2,1)} %all-gather.6.cloned.1.call-done), kind=kLoop, calls=%fused_computation.75 | loop fusion | bytes 7864320 | tf_op jit(solution)/shard_map/slice | solution.py:62
  106.7 2.7 %copy.26 = bf16[1,1,1,1280,768]{3,4,2,1,0:T(8,128)(2,1)S(1)} copy(bf16[1,1,1,1280,768]{4,3,2,1,0:T(8,128)(2,1)} %get-tuple-element.8) | data formatting | bytes 3932160 | tf_op jit(solution)/shard_map/slice | solution.py:62
  109.4 4.0 %copy.28 = bf16[1,1,1,1280,768]{3,4,2,1,0:T(8,128)(2,1)} copy(bf16[1,1,1,1280,768]{4,3,2,1,0:T(8,128)(2,1)} %get-tuple-element.9) | data formatting | bytes 3932160 | tf_op jit(solution)/shard_map/slice | solution.py:63
  113.4 0.5 select_reduce_fusion
  113.9 0.5 fusion.2
  114.4 1.1 copy-done.1
  115.5 0.7 fusion.5
  116.4 27.9 %all-gather.4.cloned.1.call-done = bf16[768,1536]{0,1:T(8,128)(2,1)} async-done(((bf16[768,192]{0,1:T(8,128)(2,1)}), bf16[768,1536]{0,1:T(8,128)(2,1)}) %all-gather.4.cloned.1.call-update) | async-done | bytes 2359312 | tf_op jit(solution)/shard_map/all_gather | solution.py:78
  144.3 2.6 %fusion.47 = (f32[32]{0:T(128)S(1)}, f32[32,1536]{1,0:T(8,128)S(1)}) fusion(bf16[32,768]{1,0:T(8,128)(2,1)S(1)} %convert_element_type.34, bf16[768,1536]{0,1:T(8,128)(2,1)} %all-gather.4.cloned.1.call-done, f32[1536]{0:T(1024)S(1)} %reduce.2, bf16[1,1,32,1536]{3,2,1,0:T(8,128)(2,1)S(1)} %copy-done.3), kind=kOutput, calls=%fused_computation.76 | convolution fusion | flops 75694048 | bytes 2709632 | tf_op jit(solution)/shard_map/dot_general | solution.py:76
  146.9 0.2 multiply_reduce_fusion.1
  147.2 15.2 %all_gather.11 = bf16[256,1536]{1,0:T(8,128)(2,1)S(1)} all-gather(bf16[32,1536]{1,0:T(8,128)(2,1)S(1)} %add_convert_fusion.1), channel_id=1, replica_groups=mesh['cfg'=2,'req'=8,'seq'=32] {'req'}, dimensions={0}, use_global_device_ids=true | all-gather | bytes 884736 | tf_op jit(solution)/shard_map/all_gather | solution.py:85
  162.4 3.3 %convolution_convert_fusion = bf16[256,1536]{1,0:T(8,128)(2,1)} fusion(bf16[384,1536]{1,0:T(8,128)(2,1)S(1)} %copy-done, bf16[256,1536]{1,0:T(8,128)(2,1)S(1)} %all_gather.11, bf16[1536,384]{1,0:T(8,128)(2,1)} %param.27), kind=kOutput, calls=%fused_computation.2 | convolution fusion | flops 605257728 | bytes 3932160 | tf_op jit(solution)/shard_map/dot_general | solution.py:92
  165.9 39.4 %reduce-scatter.2.cloned.1.call-done = bf16[32,1536]{1,0:T(8,128)(2,1)} async-done(((bf16[256,1536]{1,0:T(8,128)(2,1)}), bf16[32,1536]{1,0:T(8,128)(2,1)}) %reduce-scatter.2.cloned.1.call-update) | async-done | bytes 98320 | tf_op jit(solution)/shard_map/reduce_scatter | solution.py:91
  205.3 1.0 fusion.29
  206.3 1.1 multiply_reduce_fusion
  207.4 1.1 fusion.23
  208.6 4.8 %collective-permute-start = (f32[32,64]{1,0:T(8,128)S(1)}, f32[32,64]{1,0:T(8,128)S(1)}, u32[]{:S(2)}, u32[]{:S(2)}) collective-permute-start(f32[32,64]{1,0:T(8,128)S(1)} %fusion.23), channel_id=1, source_target_pairs={{0,256},{256,0},{1,257},{257,1},{2,258},{258,2},{3,259},{259,3},{4... | collective-permute-start | bytes 24584 | tf_op jit(solution)/shard_map/ppermute | solution.py:18
  214.0 4.1 %collective-permute-done = f32[32,64]{1,0:T(8,128)S(1)} collective-permute-done((f32[32,64]{1,0:T(8,128)S(1)}, f32[32,64]{1,0:T(8,128)S(1)}, u32[]{:S(2)}, u32[]{:S(2)}) %collective-permute-start) | collective-permute-done | bytes 8224 | tf_op jit(solution)/shard_map/ppermute | solution.py:18
  218.1 0.6 multiply_reduce_fusion.2
  218.7 1.4 pad_maximum_fusion
  220.1 0.6 broadcast_in_dim.39
  220.7 10.5 %all-to-all-start = ((f32[32,1,2]{2,1,0:T(1,128)}), f32[32,1,2]{2,1,0:T(1,128)S(1)}, u32[]{:S(2)}, u32[]{:S(2)}) async-start(f32[32,1,2]{2,1,0:T(1,128)} %broadcast_in_dim.39), calls=%async_computation.1 | async-start | bytes 32768 | tf_op jit(solution)/shard_map/all_to_all | solution.py:109
  231.2 0.7 bitcast_add_fusion
  231.9 7.8 %all-to-all-done = f32[32,1,2]{2,1,0:T(1,128)S(1)} async-done(((f32[32,1,2]{2,1,0:T(1,128)}), f32[32,1,2]{2,1,0:T(1,128)S(1)}, u32[]{:S(2)}, u32[]{:S(2)}) %all-to-all-start) | async-done | bytes 288 | tf_op jit(solution)/shard_map/all_to_all | solution.py:109
  239.8 0.6 slice_reduce_fusion
  (32 shorter events, 0.6 us)
Async XLA Ops:
  7.2 155.3 %copy-start = (bf16[384,1536]{1,0:T(8,128)(2,1)S(1)}, bf16[384,1536]{1,0:T(8,128)(2,1)}, u32[]{:S(2)}) copy-start(bf16[384,1536]{1,0:T(8,128)(2,1)} %param.28) | copy-start | bytes 3538948
  7.2 95.2 %all-gather.6.cloned.1.call-start = ((), (), s32[]{:S(2)}) async-start(), calls=%async_computation.4 | async-start | bytes 4055040 | tf_op jit(solution)/shard_map/all_gather | solution.py:55
  7.9 136.4 %all-gather.4.cloned.1.call-start = ((), (), s32[]{:S(2)}) async-start(), calls=%async_computation.2 | async-start | bytes 2654208 | tf_op jit(solution)/shard_map/all_gather | solution.py:78
  8.7 196.6 %reduce-scatter.2.cloned.1.call-start = ((), (), s32[]{:S(2)}) async-start(), calls=%async_computation.3 | async-start | bytes 884736 | tf_op jit(solution)/shard_map/reduce_scatter | solution.py:91
  113.9 1.6 copy-start.1
  115.5 28.8 %copy-start.3 = (bf16[1,1,32,1536]{3,2,1,0:T(8,128)(2,1)S(1)}, bf16[1,1,32,1536]{3,2,1,0:T(8,128)(2,1)}, u32[]{:S(2)}) copy-start(bf16[1,1,32,1536]{3,2,1,0:T(8,128)(2,1)} %param.18) | copy-start | bytes 294916
  162.4 3.4 %copy-start.6 = (f32[1,1,1536]{2,1,0:T(1,128)S(1)}, f32[1,1,1536]{2,1,0:T(1,128)}, u32[]{:S(2)}) copy-start(f32[1,1,1536]{2,1,0:T(1,128)} %param.23) | copy-start | bytes 18436
  162.4 3.4 %copy-start.7 = (f32[1,1,1536]{2,1,0:T(1,128)S(1)}, f32[1,1,1536]{2,1,0:T(1,128)}, u32[]{:S(2)}) copy-start(f32[1,1,1536]{2,1,0:T(1,128)} %param.24) | copy-start | bytes 18436
  162.4 3.4 %copy-start.5 = (f32[1,1,1536]{2,1,0:T(1,128)S(1)}, f32[1,1,1536]{2,1,0:T(1,128)}, u32[]{:S(2)}) copy-start(f32[1,1,1536]{2,1,0:T(1,128)} %param.25) | copy-start | bytes 18436
  162.4 45.0 %copy-start.2 = (bf16[1536,64]{0,1:T(8,128)(2,1)S(1)}, bf16[1536,64]{0,1:T(8,128)(2,1)}, u32[]{:S(2)}) copy-start(bf16[1536,64]{0,1:T(8,128)(2,1)} %param.29) | copy-start | bytes 589828
  165.8 65.4 %copy-start.4 = (f32[1,32,32]{2,1,0:T(8,128)S(1)}, f32[1,32,32]{2,1,0:T(8,128)}, u32[]{:S(2)}) copy-start(f32[1,32,32]{2,1,0:T(8,128)} %param.30) | copy-start | bytes 12292
  208.6 9.5 %collective-permute-start = (f32[32,64]{1,0:T(8,128)S(1)}, f32[32,64]{1,0:T(8,128)S(1)}, u32[]{:S(2)}, u32[]{:S(2)}) collective-permute-start(f32[32,64]{1,0:T(8,128)S(1)} %fusion.23), channel_id=1, source_target_pairs={{0,256},{256,0},{1,257},{257,1},{2,258},{258,2},{3,259},{259,3},{4... | collective-permute-start | bytes 24584 | tf_op jit(solution)/shard_map/ppermute | solution.py:18
  220.7 19.0 %all-to-all-start = ((f32[32,1,2]{2,1,0:T(1,128)}), f32[32,1,2]{2,1,0:T(1,128)S(1)}, u32[]{:S(2)}, u32[]{:S(2)}) async-start(f32[32,1,2]{2,1,0:T(1,128)} %broadcast_in_dim.39), calls=%async_computation.1 | async-start | bytes 32768 | tf_op jit(solution)/shard_map/all_to_all | solution.py:109
Sparse Core Ops, SparseCore 0:
  11.2 91.1 all-gather.5
  104.5 39.7 all-gather.3
  165.9 39.3 reduce-scatter.1
where the time goes:
time: 249 us
  waiting for transfers between devices  171 us (69%)
  between operations  17 us (7%)
  starting transfers between devices  15.4 us (6%)
  blocking collectives  15.2 us (6%)
  local copies, waits for them, and re-layouts  13.8 us (6%)
  other arithmetic  8.45 us (3%)
  matrix products  8.28 us (3%)
    all_gather x1, waiting for transfers between devices, per_device(): piece = lax.all_gather(key_vals, 'seq', axis=1, tiled=True)  89.9 us
    reduce_scatter x1, waiting for transfers between devices, per_device(): lax.psum_scatter(jnp.dot(inner, w_down, preferred_element_type=jnp.float3...  39.4 us
    all_gather x1, waiting for transfers between devices, per_device(): lax.all_gather(w_proj, 'req', axis=1, tiled=True)  27.9 us
    all_gather x1, blocking collectives, per_device(): lax.all_gather(mlp_in, 'req', axis=0, tiled=True)  15.2 us
    all_to_all x1, starting transfers between devices, per_device(): lax.all_to_all(jnp.broadcast_to(partials[None], (n_seq, 2)), 'seq', 0, 0,...  10.5 us
    all_to_all x1, waiting for transfers between devices, per_device(): lax.all_to_all(jnp.broadcast_to(partials[None], (n_seq, 2)), 'seq', 0, 0,...  7.82 us
    slice x2, local copies, waits for them, and re-layouts, per_device(): keys_here = piece[0].reshape(piece_rows, HEADS, HD)  6.95 us
  transfers between devices with their start and end apart: 5, of which 5 were waited for; matrix products, arithmetic and copies ran while one was open for 7% of the time, Pallas kernels for 0%

commit v1 on v0

--- a/solution.py
+++ b/solution.py
@@ -6,6 +6,11 @@
 HEADS = 12
 HD = 64
 guidance_weight = 4.0
+
+
+def gather_from_all(shard, axis, dim):
+    copies = jnp.concatenate([shard] * lax.axis_size(axis), axis=dim)
+    return lax.all_to_all(copies, axis, dim, dim, tiled=True)
 
 
 def swapped(block, axis, apart):
@@ -52,7 +57,7 @@
     queries = query[0, 0].reshape(img_dev, HEADS, HD)
     key_vals = key_value[:, 0, 0]
     factor = HD ** (-0.5)
-    piece = lax.all_gather(key_vals, "seq", axis=1, tiled=True)
+    piece = gather_from_all(key_vals, "seq", 1)
     running_max = jnp.full((img_dev, HEADS), -1e30, jnp.float32)
     piece_rows = piece.shape[1]
     positions = jnp.arange(piece_rows, dtype=jnp.int32)

time: 249 us -> 280 us (1.12)
  local copies, waits for them, and re-layouts: 13.8 us -> 65.2 us
  waiting for transfers between devices: 171 us -> 137 us
  starting transfers between devices: 15.4 us -> 28.9 us
    all_gather x1 -> x0, waiting for transfers between devices: 89.9 us -> none  [per_device(): piece = lax.all_gather(key_vals, 'seq', axis=1, tiled=True)]
    all_to_all x0 -> x1, waiting for transfers between devices: none -> 86.4 us  [gather_from_all(): return lax.all_to_all(copies, axis, dim, dim, tiled=True)]
    unnamed x16 -> x57, local copies, waits for them, and re-layouts: 1.1 us -> 38.2 us
    all_gather x1, waiting for transfers between devices: 27.9 us -> 0.02 us  [per_device(): lax.all_gather(w_proj, 'req', axis=1, tiled=True)]
    all_to_all x0 -> x1, starting transfers between devices: none -> 13.7 us  [gather_from_all(): return lax.all_to_all(copies, axis, dim, dim, tiled=True)]
    slice x2, local copies, waits for them, and re-layouts: 6.95 us -> 16.7 us  [per_device(): keys_here = piece[0].reshape(piece_rows, HEADS, HD)]
    slice x1, local copies, waits for them, and re-layouts: 4.01 us -> 8.63 us  [per_device(): vals_here = piece[1].reshape(piece_rows, HEADS, HD)]
  transfers between devices with their start and end apart: 5 -> 5, of which waited for: 5 -> 4; matrix products, arithmetic and copies ran while one was open for 7% -> 10% of each run, Pallas kernels for 0% -> 0%
where the time goes in v1:
time: 280 us; the launch traced here: 279 us
  waiting for transfers between devices  137 us (49%)
  local copies, waits for them, and re-layouts  65.2 us (23%)
  starting transfers between devices  28.9 us (10%)
  between operations  17.5 us (6%)
  blocking collectives  15.8 us (6%)
  matrix products  8.22 us (3%)
  other arithmetic  6.36 us (2%)
    all_to_all x1, waiting for transfers between devices, gather_from_all(): return lax.all_to_all(copies, axis, dim, dim, tiled=True)  86.4 us
    unnamed x57, local copies, waits for them, and re-layouts  38.2 us
    reduce_scatter x1, waiting for transfers between devices, per_device(): lax.psum_scatter(jnp.dot(inner, w_down, preferred_element_type=jnp.float3...  38.1 us
    slice x2, local copies, waits for them, and re-layouts, per_device(): keys_here = piece[0].reshape(piece_rows, HEADS, HD)  16.7 us
    all_gather x1, blocking collectives, per_device(): lax.all_gather(mlp_in, 'req', axis=0, tiled=True)  15.8 us
    all_to_all x1, starting transfers between devices, gather_from_all(): return lax.all_to_all(copies, axis, dim, dim, tiled=True)  13.7 us
    all_to_all x1, starting transfers between devices, per_device(): lax.all_to_all(jnp.broadcast_to(partials[None], (n_seq, 2)), 'seq', 0, 0,...  10.5 us
    slice x1, local copies, waits for them, and re-layouts, per_device(): vals_here = piece[1].reshape(piece_rows, HEADS, HD)  8.63 us
  transfers between devices with their start and end apart: 5, of which 4 were waited for; matrix products, arithmetic and copies ran while one was open for 10% of the time, Pallas kernels for 0%

profile of v1, /device:TPU:2, one launch (start us, length us, event | category | flops | bytes accessed | tf_op | source)
XLA Modules:
  0.0 279.2 jit_solution(7041771803221905791)
XLA Ops:
  7.2 1.8 bitcast_dynamic-update-slice_fusion.30
  8.9 1.7 bitcast_dynamic-update-slice_fusion.29
  10.6 1.6 bitcast_dynamic-update-slice_fusion.28
  12.2 1.6 bitcast_dynamic-update-slice_fusion.27
  13.9 1.6 bitcast_dynamic-update-slice_fusion.26
  15.5 1.6 bitcast_dynamic-update-slice_fusion.25
  17.2 1.6 bitcast_dynamic-update-slice_fusion.24
  18.8 1.6 bitcast_dynamic-update-slice_fusion.23
  20.4 1.6 bitcast_dynamic-update-slice_fusion.22
  22.1 1.6 bitcast_dynamic-update-slice_fusion.21
  23.7 1.6 bitcast_dynamic-update-slice_fusion.20
  25.4 1.6 bitcast_dynamic-update-slice_fusion.19
  27.0 1.6 bitcast_dynamic-update-slice_fusion.18
  28.7 1.7 bitcast_dynamic-update-slice_fusion.17
  30.3 1.6 bitcast_dynamic-update-slice_fusion.16
  32.0 1.6 bitcast_dynamic-update-slice_fusion.15
  45.5 13.7 %all-to-all-start = ((bf16[2,1280,768]{2,0,1:T(2,128)(2,1)}), bf16[2,1280,768]{2,0,1:T(2,128)(2,1)}, u32[]{:S(2)}, u32[]{:S(2)}) async-start(bf16[2,1280,768]{2,0,1:T(2,128)(2,1)} %bitcast_dynamic-update-slice_fusion.31), calls=%async_computation | async-start | bytes 7864320 | tf_op jit(solution)/shard_map/all_to_all | solution.py:13
  60.9 86.4 %all-to-all-done = bf16[2,1280,768]{2,0,1:T(2,128)(2,1)} async-done(((bf16[2,1280,768]{2,0,1:T(2,128)(2,1)}), bf16[2,1280,768]{2,0,1:T(2,128)(2,1)}, u32[]{:S(2)}, u32[]{:S(2)}) %all-to-all-start) | async-done | bytes 3932192 | tf_op jit(solution)/shard_map/all_to_all | solution.py:13
  147.4 9.4 %fusion.46 = (bf16[1,1280,768]{2,0,1:T(2,128)(2,1)}, bf16[1,1280,768]{2,0,1:T(2,128)(2,1)}) fusion(bf16[2,1280,768]{2,0,1:T(2,128)(2,1)} %all-to-all-done), kind=kLoop, calls=%fused_computation.107 | loop fusion | bytes 7864320 | tf_op jit(solution)/shard_map/slice | solution.py:67
  156.8 7.2 %copy.28 = bf16[1,1280,768]{1,2,0:T(8,128)(2,1)S(1)} copy(bf16[1,1280,768]{2,0,1:T(2,128)(2,1)} %get-tuple-element.8) | data formatting | bytes 3932160 | tf_op jit(solution)/shard_map/slice | solution.py:67
  164.0 8.6 %copy.27 = bf16[1,1280,768]{1,2,0:T(8,128)(2,1)} copy(bf16[1,1280,768]{2,0,1:T(2,128)(2,1)} %get-tuple-element.9) | data formatting | bytes 3932160 | tf_op jit(solution)/shard_map/slice | solution.py:68
  175.1 2.6 fusion.47
  178.1 15.8 %all_gather.7 = bf16[256,1536]{1,0:T(8,128)(2,1)S(1)} all-gather(bf16[32,1536]{1,0:T(8,128)(2,1)S(1)} %add_convert_fusion.1), channel_id=1, replica_groups=mesh['cfg'=2,'req'=8,'seq'=32] {'req'}, dimensions={0}, use_global_device_ids=true | all-gather | bytes 884736 | tf_op jit(solution)/shard_map/all_gather | solution.py:90
  193.9 3.3 %convolution_convert_fusion = bf16[256,1536]{1,0:T(8,128)(2,1)} fusion(bf16[384,1536]{1,0:T(8,128)(2,1)S(1)} %copy-done, bf16[256,1536]{1,0:T(8,128)(2,1)S(1)} %all_gather.7, bf16[1536,384]{1,0:T(8,128)(2,1)} %param.27), kind=kOutput, calls=%fused_computation.2 | convolution fusion | flops 605257728 | bytes 3932160 | tf_op jit(solution)/shard_map/dot_general | solution.py:97
  197.3 38.1 %reduce-scatter.2.cloned.1.call-done = bf16[32,1536]{1,0:T(8,128)(2,1)} async-done(((bf16[256,1536]{1,0:T(8,128)(2,1)}), bf16[32,1536]{1,0:T(8,128)(2,1)}) %reduce-scatter.2.cloned.1.call-update) | async-done | bytes 98320 | tf_op jit(solution)/shard_map/reduce_scatter | solution.py:96
  236.5 1.1 multiply_reduce_fusion
  237.6 1.1 fusion.23
  238.7 4.6 %collective-permute-start = (f32[32,64]{1,0:T(8,128)S(1)}, f32[32,64]{1,0:T(8,128)S(1)}, u32[]{:S(2)}, u32[]{:S(2)}) collective-permute-start(f32[32,64]{1,0:T(8,128)S(1)} %fusion.23), channel_id=1, source_target_pairs={{0,256},{256,0},{1,257},{257,1},{2,258},{258,2},{3,259},{259,3},{4... | collective-permute-start | bytes 24584 | tf_op jit(solution)/shard_map/ppermute | solution.py:23
  244.0 4.2 %collective-permute-done = f32[32,64]{1,0:T(8,128)S(1)} collective-permute-done((f32[32,64]{1,0:T(8,128)S(1)}, f32[32,64]{1,0:T(8,128)S(1)}, u32[]{:S(2)}, u32[]{:S(2)}) %collective-permute-start) | collective-permute-done | bytes 8224 | tf_op jit(solution)/shard_map/ppermute | solution.py:23
  248.8 1.4 pad_maximum_fusion
  250.8 10.5 %all-to-all-start.1 = ((f32[32,1,2]{2,1,0:T(1,128)}), f32[32,1,2]{2,1,0:T(1,128)S(1)}, u32[]{:S(2)}, u32[]{:S(2)}) async-start(f32[32,1,2]{2,1,0:T(1,128)} %broadcast_in_dim.39), calls=%async_computation.2 | async-start | bytes 32768 | tf_op jit(solution)/shard_map/all_to_all | solution.py:114
  262.0 7.8 %all-to-all-done.1 = f32[32,1,2]{2,1,0:T(1,128)S(1)} async-done(((f32[32,1,2]{2,1,0:T(1,128)}), f32[32,1,2]{2,1,0:T(1,128)S(1)}, u32[]{:S(2)}, u32[]{:S(2)}) %all-to-all-start.1) | async-done | bytes 288 | tf_op jit(solution)/shard_map/all_to_all | solution.py:114
  (73 shorter events, 19.4 us)
Async XLA Ops:
  7.2 186.7 %copy-start = (bf16[384,1536]{1,0:T(8,128)(2,1)S(1)}, bf16[384,1536]{1,0:T(8,128)(2,1)}, u32[]{:S(2)}) copy-start(bf16[384,1536]{1,0:T(8,128)(2,1)} %param.28) | copy-start | bytes 3538948
  7.2 26.4 %copy-start.1 = (bf16[2,1,1,40,768]{4,3,2,1,0:T(8,128)(2,1)S(1)}, bf16[2,1,1,40,768]{4,3,2,1,0:T(8,128)(2,1)}, u32[]{:S(2)}) copy-start(bf16[2,1,1,40,768]{4,3,2,1,0:T(8,128)(2,1)} %param.17) | copy-start | bytes 368644
  45.5 15.1 %copy-start.5 = (bf16[1,1,32,768]{3,2,1,0:T(8,128)(2,1)S(1)}, bf16[1,1,32,768]{3,2,1,0:T(8,128)(2,1)}, u32[]{:S(2)}) copy-start(bf16[1,1,32,768]{3,2,1,0:T(8,128)(2,1)} %param.16) | copy-start | bytes 147460
  45.5 15.3 %copy-start.9 = (f32[1,1,1536]{2,1,0:T(1,128)S(1)}, f32[1,1,1536]{2,1,0:T(1,128)}, u32[]{:S(2)}) copy-start(f32[1,1,1536]{2,1,0:T(1,128)} %param.20) | copy-start | bytes 18436
  45.5 15.3 %copy-start.10 = (f32[1,1,1536]{2,1,0:T(1,128)S(1)}, f32[1,1,1536]{2,1,0:T(1,128)}, u32[]{:S(2)}) copy-start(f32[1,1,1536]{2,1,0:T(1,128)} %param.21) | copy-start | bytes 18436
  45.5 15.4 %copy-start.7 = (f32[1,1,1536]{2,1,0:T(1,128)S(1)}, f32[1,1,1536]{2,1,0:T(1,128)}, u32[]{:S(2)}) copy-start(f32[1,1,1536]{2,1,0:T(1,128)} %param.22) | copy-start | bytes 18436
  45.5 101.8 %all-to-all-start = ((bf16[2,1280,768]{2,0,1:T(2,128)(2,1)}), bf16[2,1280,768]{2,0,1:T(2,128)(2,1)}, u32[]{:S(2)}, u32[]{:S(2)}) async-start(bf16[2,1280,768]{2,0,1:T(2,128)(2,1)} %bitcast_dynamic-update-slice_fusion.31), calls=%async_computation | async-start | bytes 7864320 | tf_op jit(solution)/shard_map/all_to_all | solution.py:13
  59.2 115.9 %all-gather.2.cloned.1.call-start = ((), (), s32[]{:S(2)}) async-start(), calls=%async_computation.3 | async-start | bytes 2654208 | tf_op jit(solution)/shard_map/all_gather | solution.py:83
  59.9 175.5 %reduce-scatter.2.cloned.1.call-start = ((), (), s32[]{:S(2)}) async-start(), calls=%async_computation.4 | async-start | bytes 884736 | tf_op jit(solution)/shard_map/reduce_scatter | solution.py:96
  172.7 1.5 copy-start.2
  173.2 1.9 copy-start.4
  177.7 19.5 %copy-start.11 = (f32[1,1,1536]{2,1,0:T(1,128)S(1)}, f32[1,1,1536]{2,1,0:T(1,128)}, u32[]{:S(2)}) copy-start(f32[1,1,1536]{2,1,0:T(1,128)} %param.23) | copy-start | bytes 18436
  177.7 19.5 %copy-start.12 = (f32[1,1,1536]{2,1,0:T(1,128)S(1)}, f32[1,1,1536]{2,1,0:T(1,128)}, u32[]{:S(2)}) copy-start(f32[1,1,1536]{2,1,0:T(1,128)} %param.24) | copy-start | bytes 18436
  177.7 19.5 %copy-start.8 = (f32[1,1,1536]{2,1,0:T(1,128)S(1)}, f32[1,1,1536]{2,1,0:T(1,128)}, u32[]{:S(2)}) copy-start(f32[1,1,1536]{2,1,0:T(1,128)} %param.25) | copy-start | bytes 18436
  177.8 59.8 %copy-start.3 = (bf16[1536,64]{0,1:T(8,128)(2,1)S(1)}, bf16[1536,64]{0,1:T(8,128)(2,1)}, u32[]{:S(2)}) copy-start(bf16[1536,64]{0,1:T(8,128)(2,1)} %param.29) | copy-start | bytes 589828
  178.0 83.4 %copy-start.6 = (f32[1,32,32]{2,1,0:T(8,128)S(1)}, f32[1,32,32]{2,1,0:T(8,128)}, u32[]{:S(2)}) copy-start(f32[1,32,32]{2,1,0:T(8,128)} %param.30) | copy-start | bytes 12292
  238.7 9.5 %collective-permute-start = (f32[32,64]{1,0:T(8,128)S(1)}, f32[32,64]{1,0:T(8,128)S(1)}, u32[]{:S(2)}, u32[]{:S(2)}) collective-permute-start(f32[32,64]{1,0:T(8,128)S(1)} %fusion.23), channel_id=1, source_target_pairs={{0,256},{256,0},{1,257},{257,1},{2,258},{258,2},{3,259},{259,3},{4... | collective-permute-start | bytes 24584 | tf_op jit(solution)/shard_map/ppermute | solution.py:23
  250.8 19.0 %all-to-all-start.1 = ((f32[32,1,2]{2,1,0:T(1,128)}), f32[32,1,2]{2,1,0:T(1,128)S(1)}, u32[]{:S(2)}, u32[]{:S(2)}) async-start(f32[32,1,2]{2,1,0:T(1,128)} %broadcast_in_dim.39), calls=%async_computation.2 | async-start | bytes 32768 | tf_op jit(solution)/shard_map/all_to_all | solution.py:114
Sparse Core Ops, SparseCore 0:
  62.1 43.7 all-gather.1
  197.3 38.0 reduce-scatter.1
